TPU v7x, 256 devices: a whole 4x4x8 slice. The times are simulated.
256 devices in a mesh: blk: 32 (over x, y, core), row: 8 (over z).
Axes of the slice: x: 4, y: 4, z: 8, core: 2. Of those that a mesh axis runs over, the one named last changes fastest.
Arguments:
- samples: bfloat16 [1024, 8192], P('blk', 'row'), may hold values from -8 to 8, as said below
- blocks: int32 [64, 4], replicated, may hold values from 0 to 31
- factor: float32 [64, 1024], P(None, 'row'), may hold values from -1.2 to 1.2
Outputs:
- cumulants: float32 [64, 1024, 1024], P('blk', 'row')
- factor_out: float32 [64, 1024], P(None, 'row')
Inputs may be any that keep to these rules, and one draw needn't show every extreme that they name: `samples`: channel values are drawn with mean zero.
All inputs are finite; a program needn't handle non-finite values.
Results may differ from a plain program's by a relative error of at most 0.0014.
Values may be sent and summed in bfloat16 or wider, within the bound.
No kernel may reach another device: no remote copies, remote signals or barrier semaphores. Data moves between devices by JAX's collectives and lax.ppermute only.
A program may use at most 64 MiB of HBM per device.

v0:
```python
import jax
import jax.numpy as jnp
from jax import lax
from jax.sharding import PartitionSpec as P

CHANNELS = 1024
BLOCK = 32
RANK = 64
SAMPLES = 8192
ITERS = 2
step_size = 0.2


def pair_rows(left, right):
    product = left[:, None, :].astype(jnp.float32) * right[None, :, :].astype(jnp.float32)
    return product.reshape(left.shape[0] * right.shape[0], left.shape[1]).astype(jnp.bfloat16)


def contract_last(left, right):
    return lax.dot_general(
        left, right, (((1,), (1,)), ((), ())), preferred_element_type=jnp.float32
    )


def gauss_terms(gram, count, width, row_lo):
    highest = lax.Precision.HIGHEST

    def part(first, second):
        return gram[first * width : (first + 1) * width, second * width : (second + 1) * width]

    cov_ab = lax.dynamic_slice_in_dim(part(0, 1), row_lo, count, 0)
    cov_ac = lax.dynamic_slice_in_dim(part(0, 2), row_lo, count, 0)
    cov_ad = lax.dynamic_slice_in_dim(part(0, 3), row_lo, count, 0)
    cov_cd = part(2, 3)
    cov_bd = part(1, 3)
    cov_bc = part(1, 2)
    first_term = cov_ab.reshape(-1)[:, None] * cov_cd.reshape(-1)[None, :]
    second_term = jnp.einsum("ik,jl->ijkl", cov_ac, cov_bd, precision=highest).reshape(
        count * width, width * width
    )
    third_term = jnp.einsum("il,jk->ijkl", cov_ad, cov_bc, precision=highest).reshape(
        count * width, width * width
    )
    return first_term + second_term + third_term


def add_cols(total, piece, start):
    old = lax.dynamic_slice_in_dim(total, start, piece.shape[1], 1)
    return lax.dynamic_update_slice_in_dim(total, old + piece, start, 1)


def add_grads(total, kslab, full, ids, row_lo, count, width):
    highest = lax.Precision.HIGHEST
    rank = full.shape[0]
    start_a = ids[0] * width + row_lo
    fac_a = lax.dynamic_slice_in_dim(full, start_a, count, 1)
    fac_b = lax.dynamic_slice_in_dim(full, ids[1] * width, width, 1)
    fac_c = lax.dynamic_slice_in_dim(full, ids[2] * width, width, 1)
    fac_d = lax.dynamic_slice_in_dim(full, ids[3] * width, width, 1)
    upair = (fac_a[:, :, None] * fac_b[:, None, :]).reshape(rank, count * width)
    vpair = (fac_c[:, :, None] * fac_d[:, None, :]).reshape(rank, width * width)
    model = lax.dot_general(upair, vpair, (((0,), (0,)), ((), ())), precision=highest)
    resid = kslab - model
    wmat = lax.dot_general(vpair, resid, (((1,), (1,)), ((), ())), precision=highest).reshape(
        rank, count, width
    )
    zmat = jnp.dot(upair, resid, precision=highest).reshape(rank, width, width)
    total = add_cols(total, jnp.sum(wmat * fac_b[:, None, :], axis=2), start_a)
    total = add_cols(total, jnp.sum(wmat * fac_a[:, :, None], axis=1), ids[1] * width)
    total = add_cols(total, jnp.sum(zmat * fac_d[:, None, :], axis=2), ids[2] * width)
    total = add_cols(total, jnp.sum(zmat * fac_c[:, :, None], axis=1), ids[3] * width)
    return total


def gather_factor(columns):
    return lax.all_gather(columns, "row", axis=1, tiled=True)


def per_device(samples, blocks, factor):
    width = BLOCK
    row_count = lax.axis_size("row")
    count = width // row_count
    row_lo = lax.axis_index("row") * count
    per_owner = blocks.shape[0] // lax.axis_size("blk")
    mine = lax.dynamic_slice_in_dim(blocks, lax.axis_index("blk") * per_owner, per_owner, 0)
    needed = mine.reshape(-1)
    pairs = width * width
    piece = lax.all_gather(samples, "blk", axis=0, tiled=True)
    pieces = piece.shape[0] // width
    owned = jnp.arange(pieces, dtype=jnp.int32)
    select = (needed[:, None] == owned[None, :]).astype(jnp.bfloat16)
    shaped = piece.reshape(pieces, width, piece.shape[1])
    taken = jnp.einsum("mb,bcs->mcs", select, shaped, preferred_element_type=jnp.float32)
    local = taken.astype(jnp.bfloat16)
    slabs = []
    whole = lax.all_gather(local, "row", axis=2, tiled=True)
    sample_block = min(SAMPLES, 2048)
    for slot in range(per_owner):
        source_a = whole[4 * slot]
        source_b = whole[4 * slot + 1]
        source_c = whole[4 * slot + 2]
        source_d = whole[4 * slot + 3]

        def accumulate(index, moment):
            low = index * sample_block
            left = lax.dynamic_slice(source_a, (row_lo, low), (count, sample_block))
            right = lax.dynamic_slice_in_dim(source_b, low, sample_block, 1)
            third = lax.dynamic_slice_in_dim(source_c, low, sample_block, 1)
            fourth = lax.dynamic_slice_in_dim(source_d, low, sample_block, 1)
            pmat = pair_rows(left, right)
            qmat = pair_rows(third, fourth)
            return moment + contract_last(pmat, qmat)

        moment = lax.fori_loop(
            0, SAMPLES // sample_block, accumulate, jnp.zeros((count * width, pairs), jnp.float32)
        )
        moment = moment / SAMPLES
        joined = whole[4 * slot : 4 * slot + 4].reshape(4 * width, whole.shape[2])
        gram = contract_last(joined, joined) / SAMPLES
        slabs.append(moment - gauss_terms(gram, count, width, row_lo))
    columns = factor
    full = gather_factor(columns)
    for step in range(ITERS):
        grad = jnp.zeros(full.shape, jnp.float32)
        for slot in range(per_owner):
            grad = add_grads(grad, slabs[slot], full, mine[slot], row_lo, count, width)
        owned_cols = lax.psum_scatter(grad, "row", scatter_dimension=1, tiled=True)
        owned_cols = lax.psum(owned_cols, "blk")
        squares = lax.psum(jnp.sum(owned_cols * owned_cols), "row")
        scale = lax.rsqrt(squares / (RANK * CHANNELS) + 1e-06)
        columns = columns + step_size * scale * owned_cols
        if step + 1 < ITERS:
            full = gather_factor(columns)
    return (jnp.stack(slabs), columns)


def solution(mesh):
    placed = (P("blk", "row"), P(), P(None, "row"))
    return jax.shard_map(
        per_device,
        mesh=mesh,
        in_specs=placed,
        out_specs=(P("blk", "row", None), P(None, "row")),
        check_vma=False,
    )
```

profile of v0, /device:TPU:32, one launch (start us, length us, event | category | flops | bytes accessed | tf_op | source)
XLA Modules:
  0.0 646.9 jit_solution(17991353607669108797)
XLA Ops:
  8.2 53.5 %all-gather.3.cloned.1.call-done = bf16[1024,1024]{1,0:T(8,128)(2,1)} async-done(((bf16[32,1024]{1,0:T(8,128)(2,1)}), bf16[1024,1024]{1,0:T(8,128)(2,1)}) %all-gather.3.cloned.1.call-update) | async-done | bytes 2097168 | tf_op jit(solution)/shard_map/all_gather | solution.py:88
  61.8 4.7 fusion.2
  72.3 26.5 %all_gather.14 = f32[64,1024]{1,0:T(8,128)S(1)} all-gather(f32[64,128]{1,0:T(8,128)S(1)} %copy-done.11), channel_id=1, replica_groups=mesh['blk'=32,'row'=8] {'row'}, dimensions={1}, use_global_device_ids=true | all-gather | bytes 294912 | tf_op jit(solution)/shard_map/all_gather | solution.py:76
  101.3 19.8 %all-gather.5.cloned.1.call-done = bf16[8,32,8192]{2,0,1:T(8,128)(2,1)} async-done(((bf16[8,32,1024]{2,0,1:T(8,128)(2,1)}), bf16[8,32,8192]{2,0,1:T(8,128)(2,1)}) %all-gather.5.cloned.1.call-update) | async-done | bytes 4194320 | tf_op jit(solution)/shard_map/all_gather | solution.py:96
  121.1 21.7 %fusion.10 = (bf16[1,32,8192]{2,0,1:T(2,128)(2,1)S(1)}, bf16[1,32,8192]{2,0,1:T(2,128)(2,1)}, bf16[1,32,8192]{2,0,1:T(2,128)(2,1)}, bf16[1,32,8192]{2,0,1:T(2,12...) fusion(bf16[8,32,8192]{2,0,1:T(8,128)(2,1)} %all-gather.5.clone, ...), kind=kLoop, calls=%fused_computation.112 | loop fusion | bytes 8388608 | tf_op jit(solution)/shard_map/slice | solution.py:102
  142.8 2.0 copy_bitcast_fusion.6
  144.8 1.1 copy_bitcast_fusion.4
  145.9 31.4 %while.32 = (s32[]{:T(128)}, f32[128,1024]{1,0:T(8,128)S(1)}, bf16[32,8192]{1,0:T(8,128)(2,1)}, s32[]{:T(128)}, bf16[32,8192]{1,0:T(8,128)(2,1)S(1)}, /*index=5*...) while((s32[]{:T(128)}, f32[128,1024]{1,0:T(8,128)S(1)}, ...), condition=%wide.region_1.0_spmd.clone, body=%wide.region_0.0_spmd.clone.sunk | while | flops 542056448 | bytes 12533941 | solution.py:114
  146.0 3.0 multiply_convert_fusion.9
  150.0 3.8 convolution_add_fusion.4
  153.9 3.0 multiply_convert_fusion.9
  157.9 3.8 convolution_add_fusion.4
  161.7 3.0 multiply_convert_fusion.9
  165.7 3.8 convolution_add_fusion.4
  169.6 3.0 multiply_convert_fusion.9
  173.6 3.8 convolution_add_fusion.4
  177.4 6.7 %fusion.11 = (bf16[4,32,8192]{2,0,1:T(4,128)(2,1)S(1)}, bf16[4,32,8192]{2,0,1:T(4,128)(2,1)}) fusion(bf16[8,32,8192]{2,0,1:T(8,128)(2,1)} %all-gather.5.cloned.1.call-done), kind=kLoop, calls=%fused_computation.113 | loop fusion | bytes 8388608 | tf_op jit(solution)/shard_map/slice | solution.py:118
  184.0 1.2 copy.68
  186.9 1.8 reshape.324
  188.7 2.7 copy.69
  192.6 1.8 reshape.325
  194.5 1.4 add_subtract_fusion.1
  196.5 1.0 copy.75
  197.6 3.6 copy_bitcast_fusion.2
  201.1 2.1 copy_bitcast_fusion
  203.3 35.3 %while.33 = (s32[]{:T(128)}, f32[128,1024]{1,0:T(8,128)S(1)}, bf16[32,8192]{1,0:T(8,128)(2,1)}, s32[]{:T(128)}, bf16[32,8192]{1,0:T(8,128)(2,1)S(1)}, /*index=5*...) while((s32[]{:T(128)}, f32[128,1024]{1,0:T(8,128)S(1)}, ...), condition=%wide.region_3.0_spmd.clone, body=%wide.region_2.0_spmd.clone.sunk | while | flops 542056448 | bytes 12533941 | solution.py:114
  204.3 3.0 multiply_convert_fusion.11
  208.2 3.8 convolution_add_fusion.5
  213.0 3.0 multiply_convert_fusion.11
  217.0 3.8 convolution_add_fusion.5
  221.8 3.0 multiply_convert_fusion.11
  225.8 3.8 convolution_add_fusion.5
  230.6 3.0 multiply_convert_fusion.11
  234.6 3.8 convolution_add_fusion.5
  238.9 1.8 reshape.327
  241.0 1.8 reshape.328
  242.9 1.4 add_subtract_fusion
  245.9 1.7 multiply_reduce_fusion.6
  250.8 37.1 %reduce-scatter.3.cloned.1.call-done = f32[64,128]{0,1:T(8,128)} async-done(((f32[64,1024]{0,1:T(8,128)}), f32[64,128]{0,1:T(8,128)}) %reduce-scatter.3.cloned.1.call-update) | async-done | bytes 32784 | tf_op jit(solution)/shard_map/reduce_scatter | solution.py:127
  287.9 124.3 %psum.28 = f32[64,128]{0,1:T(8,128)S(1)} all-reduce(f32[64,128]{0,1:T(8,128)} %reduce-scatter.3.cloned.1.call-done), channel_id=1, replica_groups=mesh['blk'=32,'row'=8] {'blk'}, use_global_device_ids=true, to_apply=%region_13.0 | all-reduce | flops 8192 | bytes 65536 | tf_op jit(solution)/shard_map/psum | solution.py:128
  412.9 16.0 %psum.29 = f32[]{:T(128)} all-reduce(f32[]{:T(128)} %multiply_reduce_fusion.13), channel_id=1, replica_groups=mesh['blk'=32,'row'=8] {'row'}, use_global_device_ids=true, to_apply=%region_15.0 | all-reduce | flops 1 | bytes 8 | tf_op jit(solution)/shard_map/psum | solution.py:129
  429.7 24.3 %all_gather.15 = f32[64,1024]{0,1:T(8,128)S(1)} all-gather(f32[64,128]{0,1:T(8,128)S(1)} %multiply_add_fusion.1), channel_id=1, replica_groups=mesh['blk'=32,'row'=8] {'row'}, dimensions={1}, use_global_device_ids=true | all-gather | bytes 294912 | tf_op jit(solution)/shard_map/all_gather | solution.py:76
  457.3 1.7 multiply_reduce_fusion
  459.7 1.7 multiply_reduce_fusion.2
  463.1 34.0 %reduce-scatter.5.cloned.1.call-done = f32[64,128]{0,1:T(8,128)} async-done(((f32[64,1024]{0,1:T(8,128)}), f32[64,128]{0,1:T(8,128)}) %reduce-scatter.5.cloned.1.call-update) | async-done | bytes 32784 | tf_op jit(solution)/shard_map/reduce_scatter | solution.py:127
  497.1 124.3 %psum.30 = f32[64,128]{0,1:T(8,128)S(1)} all-reduce(f32[64,128]{0,1:T(8,128)} %reduce-scatter.5.cloned.1.call-done), channel_id=1, replica_groups=mesh['blk'=32,'row'=8] {'blk'}, use_global_device_ids=true, to_apply=%region_25.0 | all-reduce | flops 8192 | bytes 65536 | tf_op jit(solution)/shard_map/psum | solution.py:128
  622.0 1.0 pad_maximum_fusion
  623.1 15.9 %psum.31 = f32[]{:T(128)} all-reduce(f32[]{:T(128)} %multiply_reduce_fusion.8), channel_id=1, replica_groups=mesh['blk'=32,'row'=8] {'row'}, use_global_device_ids=true, to_apply=%region_27.0 | all-reduce | flops 1 | bytes 8 | tf_op jit(solution)/shard_map/psum | solution.py:129
  (143 shorter events, 32.7 us)
Async XLA Ops:
  7.2 0.8 copy-start
  7.2 65.1 %copy-start.11 = (f32[64,128]{1,0:T(8,128)S(1)}, f32[64,128]{1,0:T(8,128)}, u32[]{:S(2)}) copy-start(f32[64,128]{1,0:T(8,128)} %param.9) | copy-start | bytes 98308
  7.2 54.6 %all-gather.3.cloned.1.call-start = ((), (), s32[]{:S(2)}) async-start(), calls=%async_computation.2 | async-start | bytes 2162688 | tf_op jit(solution)/shard_map/all_gather | solution.py:88
  7.9 113.2 %all-gather.5.cloned.1.call-start = ((), (), s32[]{:S(2)}) async-start(), calls=%async_computation.3 | async-start | bytes 4718592 | tf_op jit(solution)/shard_map/all_gather | solution.py:96
  66.5 221.4 %reduce-scatter.3.cloned.1.call-start = ((), (), s32[]{:S(2)}) async-start(), calls=%async_computation.4 | async-start | bytes 589824 | tf_op jit(solution)/shard_map/reduce_scatter | solution.py:127
  192.3 2.1 copy-start.12
  194.4 1.5 copy-start.2
  196.5 4.6 copy-start.4
  196.5 4.6 copy-start.6
  197.6 3.6 copy-start.7
  242.8 1.5 copy-start.1
  244.3 3.4 copy-start.3
  244.3 3.4 copy-start.5
  245.9 3.3 copy-start.10
  249.9 0.8 copy-start.9
  250.7 246.3 %reduce-scatter.5.cloned.1.call-start = ((), (), s32[]{:S(2)}) async-start(), calls=%async_computation.5 | async-start | bytes 589824 | tf_op jit(solution)/shard_map/reduce_scatter | solution.py:127
  462.3 0.8 copy-start.8
Sparse Core Ops, SparseCore 0:
  10.6 51.1 all-gather.2
  66.6 54.4 all-gather.4
  250.8 36.9 reduce-scatter.2
  463.2 33.8 reduce-scatter.4
where the time goes:
time: 648 us; the launch traced here: 647 us
  blocking collectives  331 us (51%)
  waiting for transfers between devices  145 us (22%)
  local copies, waits for them, and re-layouts  57.5 us (9%)
  matrix products  47.2 us (7%)
  other arithmetic  44.2 us (7%)
  between operations  20.7 us (3%)
    psum x2, blocking collectives, per_device(): owned_cols = lax.psum(owned_cols, 'blk')  249 us
    reduce_scatter x2, waiting for transfers between devices, per_device(): owned_cols = lax.psum_scatter(grad, 'row', scatter_dimension=1, tiled=True)  71.1 us
    all_gather x1, waiting for transfers between devices, per_device(): piece = lax.all_gather(samples, 'blk', axis=0, tiled=True)  53.5 us
    all_gather x2, blocking collectives, gather_factor(): return lax.all_gather(columns, 'row', axis=1, tiled=True)  50.7 us
    psum x2, blocking collectives, per_device(): squares = lax.psum(jnp.sum(owned_cols * owned_cols), 'row')  32 us
    dot_general x10, matrix products, contract_last(): lax.dot_general(left, right, (((1,), (1,)), ((), ())), preferred_element_...  31.6 us
    convert_element_type x16, other arithmetic, pair_rows(): product.reshape(left.shape[0] * right.shape[0], left.shape[1])  24.8 us
    slice x1, local copies, waits for them, and re-layouts, per_device(): source_d = whole[4 * slot + 3]  21.7 us
  transfers between devices with their start and end apart: 4, of which 4 were waited for; matrix products, arithmetic and copies ran while one was open for 1% of the time, Pallas kernels for 0%

commit v1 on v0

--- a/solution.py
+++ b/solution.py
@@ -125,7 +125,7 @@
         for slot in range(per_owner):
             grad = add_grads(grad, slabs[slot], full, mine[slot], row_lo, count, width)
         owned_cols = lax.psum_scatter(grad, "row", scatter_dimension=1, tiled=True)
-        owned_cols = lax.psum(owned_cols, "blk")
+        owned_cols = jnp.sum(lax.all_gather(owned_cols, "blk"), axis=0)
         squares = lax.psum(jnp.sum(owned_cols * owned_cols), "row")
         scale = lax.rsqrt(squares / (RANK * CHANNELS) + 1e-06)
         columns = columns + step_size * scale * owned_cols

time: 648 us -> 508 us (0.78)
  blocking collectives: 331 us -> 84.1 us
  waiting for transfers between devices: 145 us -> 244 us
    psum x2 -> x0, blocking collectives: 249 us -> none  [per_device(): owned_cols = lax.psum(owned_cols, 'blk')]
    all_gather x0 -> x2, waiting for transfers between devices: none -> 96.6 us  [per_device(): owned_cols = jnp.sum(lax.all_gather(owned_cols, 'blk'), axis=0)]
  transfers between devices with their start and end apart: 4 -> 6, of which waited for: 4 -> 6; matrix products, arithmetic and copies ran while one was open for 1% -> 1% of each run, Pallas kernels for 0% -> 0%
where the time goes in v1:
time: 508 us; the launch traced here: 505 us
  waiting for transfers between devices  244 us (48%)
  blocking collectives  84.1 us (17%)
  local copies, waits for them, and re-layouts  60.5 us (12%)
  other arithmetic  47.4 us (9%)
  matrix products  47.2 us (9%)
  between operations  21 us (4%)
    all_gather x2, waiting for transfers between devices, per_device(): owned_cols = jnp.sum(lax.all_gather(owned_cols, 'blk'), axis=0)  96.6 us
    reduce_scatter x2, waiting for transfers between devices, per_device(): owned_cols = lax.psum_scatter(grad, 'row', scatter_dimension=1, tiled=True)  72.9 us
    all_gather x1, waiting for transfers between devices, per_device(): piece = lax.all_gather(samples, 'blk', axis=0, tiled=True)  53.5 us
    all_gather x2, blocking collectives, gather_factor(): return lax.all_gather(columns, 'row', axis=1, tiled=True)  50.8 us
    psum x2, blocking collectives, per_device(): squares = lax.psum(jnp.sum(owned_cols * owned_cols), 'row')  33.4 us
    dot_general x10, matrix products, contract_last(): lax.dot_general(left, right, (((1,), (1,)), ((), ())), preferred_element_...  31.6 us
    convert_element_type x16, other arithmetic, pair_rows(): product.reshape(left.shape[0] * right.shape[0], left.shape[1])  24.8 us
    slice x1, local copies, waits for them, and re-layouts, per_device(): source_d = whole[4 * slot + 3]  21.7 us
  transfers between devices with their start and end apart: 6, of which 6 were waited for; matrix products, arithmetic and copies ran while one was open for 1% of the time, Pallas kernels for 0%

profile of v1, /device:TPU:32, one launch (start us, length us, event | category | flops | bytes accessed | tf_op | source)
XLA Modules:
  0.0 504.9 jit_solution(14885071330593108397)
XLA Ops:
  8.2 53.5 %all-gather.7.cloned.1.call-done = bf16[1024,1024]{1,0:T(8,128)(2,1)} async-done(((bf16[32,1024]{1,0:T(8,128)(2,1)}), bf16[1024,1024]{1,0:T(8,128)(2,1)}) %all-gather.7.cloned.1.call-update) | async-done | bytes 2097168 | tf_op jit(solution)/shard_map/all_gather | solution.py:88
  61.8 4.7 fusion.2
  72.3 26.5 %all_gather.26 = f32[64,1024]{1,0:T(8,128)S(1)} all-gather(f32[64,128]{1,0:T(8,128)S(1)} %copy-done.11), channel_id=1, replica_groups=mesh['blk'=32,'row'=8] {'row'}, dimensions={1}, use_global_device_ids=true | all-gather | bytes 294912 | tf_op jit(solution)/shard_map/all_gather | solution.py:76
  101.3 19.8 %all-gather.9.cloned.1.call-done = bf16[8,32,8192]{2,0,1:T(8,128)(2,1)} async-done(((bf16[8,32,1024]{2,0,1:T(8,128)(2,1)}), bf16[8,32,8192]{2,0,1:T(8,128)(2,1)}) %all-gather.9.cloned.1.call-update) | async-done | bytes 4194320 | tf_op jit(solution)/shard_map/all_gather | solution.py:96
  121.1 21.7 %fusion.10 = (bf16[1,32,8192]{2,0,1:T(2,128)(2,1)S(1)}, bf16[1,32,8192]{2,0,1:T(2,128)(2,1)}, bf16[1,32,8192]{2,0,1:T(2,128)(2,1)}, bf16[1,32,8192]{2,0,1:T(2,12...) fusion(bf16[8,32,8192]{2,0,1:T(8,128)(2,1)} %all-gather.9.clone, ...), kind=kLoop, calls=%fused_computation.112 | loop fusion | bytes 8388608 | tf_op jit(solution)/shard_map/slice | solution.py:102
  142.8 2.0 copy_bitcast_fusion.6
  145.9 31.4 %while.32 = (s32[]{:T(128)}, f32[128,1024]{1,0:T(8,128)S(1)}, bf16[32,8192]{1,0:T(8,128)(2,1)}, s32[]{:T(128)}, bf16[32,8192]{1,0:T(8,128)(2,1)S(1)}, /*index=5*...) while((s32[]{:T(128)}, f32[128,1024]{1,0:T(8,128)S(1)}, ...), condition=%wide.region_1.0_spmd.clone, body=%wide.region_0.0_spmd.clone.sunk | while | flops 542056448 | bytes 12533941 | solution.py:114
  146.0 3.0 multiply_convert_fusion.9
  150.0 3.8 convolution_add_fusion.4
  153.9 3.0 multiply_convert_fusion.9
  157.9 3.8 convolution_add_fusion.4
  161.7 3.0 multiply_convert_fusion.9
  165.7 3.8 convolution_add_fusion.4
  169.6 3.0 multiply_convert_fusion.9
  173.6 3.8 convolution_add_fusion.4
  177.4 6.7 %fusion.11 = (bf16[4,32,8192]{2,0,1:T(4,128)(2,1)S(1)}, bf16[4,32,8192]{2,0,1:T(4,128)(2,1)}) fusion(bf16[8,32,8192]{2,0,1:T(8,128)(2,1)} %all-gather.9.cloned.1.call-done), kind=kLoop, calls=%fused_computation.113 | loop fusion | bytes 8388608 | tf_op jit(solution)/shard_map/slice | solution.py:118
  186.9 1.8 reshape.324
  188.7 2.7 copy.135
  192.6 1.8 reshape.325
  194.5 1.4 add_subtract_fusion.1
  197.6 3.6 copy_bitcast_fusion.2
  201.1 2.1 copy_bitcast_fusion
  203.3 35.3 %while.33 = (s32[]{:T(128)}, f32[128,1024]{1,0:T(8,128)S(1)}, bf16[32,8192]{1,0:T(8,128)(2,1)}, s32[]{:T(128)}, bf16[32,8192]{1,0:T(8,128)(2,1)S(1)}, /*index=5*...) while((s32[]{:T(128)}, f32[128,1024]{1,0:T(8,128)S(1)}, ...), condition=%wide.region_3.0_spmd.clone, body=%wide.region_2.0_spmd.clone.sunk | while | flops 542056448 | bytes 12533941 | solution.py:114
  204.3 3.0 multiply_convert_fusion.11
  208.2 3.8 convolution_add_fusion.5
  213.0 3.0 multiply_convert_fusion.11
  217.0 3.8 convolution_add_fusion.5
  221.8 3.0 multiply_convert_fusion.11
  225.8 3.8 convolution_add_fusion.5
  230.6 3.0 multiply_convert_fusion.11
  234.6 3.8 convolution_add_fusion.5
  238.9 1.8 reshape.327
  241.0 1.8 reshape.328
  242.9 1.4 add_subtract_fusion
  245.9 1.7 multiply_reduce_fusion.6
  250.8 37.1 %reduce-scatter.3.cloned.1.call-done = f32[64,128]{0,1:T(8,128)} async-done(((f32[64,1024]{0,1:T(8,128)}), f32[64,128]{0,1:T(8,128)}) %reduce-scatter.3.cloned.1.call-update) | async-done | bytes 32784 | tf_op jit(solution)/shard_map/reduce_scatter | solution.py:127
  287.9 1.5 copy.150
  289.5 48.3 %all-gather.11.cloned.1.call-done = f32[2048,128]{1,0:T(8,128)} async-done(((f32[64,128]{1,0:T(8,128)}), f32[2048,128]{1,0:T(8,128)}) %all-gather.11.cloned.1.call-update) | async-done | bytes 1048592 | tf_op jit(solution)/shard_map/all_gather | solution.py:128
  337.8 1.3 reduce_sum.188
  339.7 16.7 %psum.14 = f32[]{:T(128)} all-reduce(f32[]{:T(128)} %multiply_reduce_fusion.17), channel_id=1, replica_groups=mesh['blk'=32,'row'=8] {'row'}, use_global_device_ids=true, to_apply=%region_15.0 | all-reduce | flops 1 | bytes 8 | tf_op jit(solution)/shard_map/psum | solution.py:129
  357.1 24.3 %all_gather.29 = f32[64,1024]{1,0:T(8,128)S(1)} all-gather(f32[64,128]{1,0:T(8,128)S(1)} %multiply_add_fusion.1), channel_id=1, replica_groups=mesh['blk'=32,'row'=8] {'row'}, dimensions={1}, use_global_device_ids=true | all-gather | bytes 294912 | tf_op jit(solution)/shard_map/all_gather | solution.py:76
  385.5 1.7 multiply_reduce_fusion
  387.9 1.7 multiply_reduce_fusion.2
  391.4 35.8 %reduce-scatter.5.cloned.1.call-done = f32[64,128]{0,1:T(8,128)} async-done(((f32[64,1024]{0,1:T(8,128)}), f32[64,128]{0,1:T(8,128)}) %reduce-scatter.5.cloned.1.call-update) | async-done | bytes 32784 | tf_op jit(solution)/shard_map/reduce_scatter | solution.py:127
  427.2 1.5 copy.165
  428.8 48.3 %all-gather.13.cloned.1.call-done = f32[2048,128]{1,0:T(8,128)} async-done(((f32[64,128]{1,0:T(8,128)}), f32[2048,128]{1,0:T(8,128)}) %all-gather.13.cloned.1.call-update) | async-done | bytes 1048592 | tf_op jit(solution)/shard_map/all_gather | solution.py:128
  477.1 1.3 reduce_sum.198
  480.0 16.7 %psum.15 = f32[]{:T(128)} all-reduce(f32[]{:T(128)} %multiply_reduce_fusion.16), channel_id=1, replica_groups=mesh['blk'=32,'row'=8] {'row'}, use_global_device_ids=true, to_apply=%region_27.0 | all-reduce | flops 1 | bytes 8 | tf_op jit(solution)/shard_map/psum | solution.py:129
  (157 shorter events, 37.7 us)
Async XLA Ops:
  7.2 0.8 copy-start
  7.2 65.1 %copy-start.11 = (f32[64,128]{1,0:T(8,128)S(1)}, f32[64,128]{1,0:T(8,128)}, u32[]{:S(2)}) copy-start(f32[64,128]{1,0:T(8,128)} %param.9) | copy-start | bytes 98308
  7.2 54.6 %all-gather.7.cloned.1.call-start = ((), (), s32[]{:S(2)}) async-start(), calls=%async_computation.2 | async-start | bytes 2162688 | tf_op jit(solution)/shard_map/all_gather | solution.py:88
  7.9 113.2 %all-gather.9.cloned.1.call-start = ((), (), s32[]{:S(2)}) async-start(), calls=%async_computation.3 | async-start | bytes 4718592 | tf_op jit(solution)/shard_map/all_gather | solution.py:96
  66.5 221.4 %reduce-scatter.3.cloned.1.call-start = ((), (), s32[]{:S(2)}) async-start(), calls=%async_computation.4 | async-start | bytes 589824 | tf_op jit(solution)/shard_map/reduce_scatter | solution.py:127
  192.3 2.1 copy-start.12
  194.4 1.5 copy-start.2
  196.5 4.6 copy-start.4
  196.5 4.6 copy-start.6
  197.6 3.6 copy-start.7
  242.8 1.5 copy-start.1
  244.3 3.4 copy-start.3
  244.3 3.4 copy-start.5
  245.9 3.3 copy-start.10
  249.9 0.8 copy-start.9
  250.7 87.1 %all-gather.11.cloned.1.call-start = ((), (), s32[]{:S(2)}) async-start(), calls=%async_computation.6 | async-start | bytes 1081344 | tf_op jit(solution)/shard_map/all_gather | solution.py:128
  289.4 137.7 %reduce-scatter.5.cloned.1.call-start = ((), (), s32[]{:S(2)}) async-start(), calls=%async_computation.5 | async-start | bytes 589824 | tf_op jit(solution)/shard_map/reduce_scatter | solution.py:127
  390.5 0.8 copy-start.8
  391.3 85.8 %all-gather.13.cloned.1.call-start = ((), (), s32[]{:S(2)}) async-start(), calls=%async_computation.7 | async-start | bytes 1081344 | tf_op jit(solution)/shard_map/all_gather | solution.py:128
Sparse Core Ops, SparseCore 0:
  10.6 51.1 all-gather.6
  66.6 54.4 all-gather.8
  250.8 36.9 reduce-scatter.2
  290.9 46.8 all-gather.10
  391.4 35.7 reduce-scatter.4
  430.2 46.8 all-gather.12
